TPU v7x, 512 devices: a whole 4x8x8 slice. The times are simulated.
512 devices in a mesh: fsdp: 128 (over z, y, core), tp: 4 (over x).
Axes of the slice: x: 4, y: 8, z: 8, core: 2. Of those that a mesh axis runs over, the one named last changes fastest.
Arguments:
- q_grad: bfloat16 [128, 1280, 768], P('fsdp', None, 'tp'), may hold values from -24 to 24, as said below
- o_grad: bfloat16 [128, 768, 1280], P('fsdp', 'tp'), may hold values from -24 to 24, as said below
- norm_grad: float32 [128, 4, 1344], P('fsdp', 'tp'), may hold values from -6 to 6, as said below
- emb_grad: bfloat16 [8192, 1280], P('fsdp', 'tp'), may hold values from -6 to 6, as said below
- flat_master: float32 [4, 491520], P('tp', 'fsdp'), may hold values from -0.15625 to 0.15625
- flat_first: float32 [4, 491520], P('tp', 'fsdp'), may hold values from -0.75 to 0.75
- flat_second: float32 [4, 491520], P('tp', 'fsdp'), may hold values from 0.001 to 0.1
- emb_master: float32 [8192, 1280], P(('fsdp', 'tp')), may hold values from -0.3125 to 0.3125
- emb_first: float32 [8192, 1280], P(('fsdp', 'tp')), may hold values from -0.75 to 0.75
- emb_second: float32 [8192, 1280], P(('fsdp', 'tp')), may hold values from 0.001 to 0.1
- norm_master: float32 [1344], replicated, may hold values from 0.5 to 1.5
- norm_first: float32 [1344], replicated, may hold values from -0.75 to 0.75
- norm_second: float32 [1344], replicated, may hold values from 0.001 to 0.1
- step_count: int32 [1], replicated, may hold values from 1 to 64
Outputs:
- new_flat_master: float32 [4, 491520], P('tp', 'fsdp')
- new_flat_first: float32 [4, 491520], P('tp', 'fsdp')
- new_flat_second: float32 [4, 491520], P('tp', 'fsdp')
- new_emb_master: float32 [8192, 1280], P(('fsdp', 'tp'))
- new_emb_first: float32 [8192, 1280], P(('fsdp', 'tp'))
- new_emb_second: float32 [8192, 1280], P(('fsdp', 'tp'))
- new_norm_master: float32 [1344], replicated
- new_norm_first: float32 [1344], replicated
- new_norm_second: float32 [1344], replicated
- q_weight: bfloat16 [1280, 768], P(None, 'tp')
- o_weight: bfloat16 [768, 1280], P('tp')
- q_average: bfloat16 [1280, 768], P('fsdp')
- o_average: bfloat16 [768, 1280], P(None, 'fsdp')
- emb_weight: bfloat16 [8192, 1280], P('fsdp', 'tp')
Inputs may be any that keep to these rules, and one draw needn't show every extreme that they name: `q_grad`: each data replica's gradient of the query projection. `o_grad`: each data replica's gradient of the output projection. `norm_grad`: each device's gradient of the gains. `emb_grad`: the embedding slice's summed gradient.
All inputs are finite; a program needn't handle non-finite values.
Results may differ from a plain program's by a relative error of at most 0.0004.
Values may be sent and summed in bfloat16 or wider, within the bound.
No kernel may reach another device: no remote copies, remote signals or barrier semaphores. Data moves between devices by JAX's collectives and lax.ppermute only.
A program may use at most 64 MiB of HBM per device.

v0:
```python
import math
import jax
import jax.numpy as jnp
from jax import lax
from jax.sharding import PartitionSpec as P

BETA_ONE = 0.9
BETA_TWO = 0.95
EPSILON = 1e-08
LEARN_RATE = 0.0053


def adam_update(weights_in, first_in, second_in, gradient, first_fix, second_fix, decay_rate):
    first_out = BETA_ONE * first_in + (1.0 - BETA_ONE) * gradient
    second_out = BETA_TWO * second_in + (1.0 - BETA_TWO) * gradient * gradient
    update = first_out / first_fix / (jnp.sqrt(second_out / second_fix) + EPSILON)
    weights_out = weights_in - LEARN_RATE * (update + decay_rate * weights_in)
    return (weights_out, first_out, second_out)


def body(
    q_grad,
    o_grad,
    norm_grad,
    emb_grad,
    flat_master,
    flat_first,
    flat_second,
    emb_master,
    emb_first,
    emb_second,
    norm_master,
    norm_first,
    norm_second,
    step_count,
):
    fsdp_count = lax.axis_size("fsdp")
    tp_count = lax.axis_size("tp")
    width = q_grad.shape[1]
    q_columns = q_grad.shape[2]
    entry_count = (
        2 * width * q_columns * tp_count
        + emb_grad.shape[0] * fsdp_count * width
        + norm_master.shape[0]
    )
    clip_limit = 0.5 * math.sqrt(entry_count)
    local_flat = jnp.concatenate([q_grad[0].reshape(-1), o_grad[0].reshape(-1)])
    piece_len = local_flat.shape[0] // fsdp_count
    summed = lax.psum(local_flat.astype(jnp.float32), "fsdp")
    grad_piece = lax.dynamic_slice_in_dim(summed, lax.axis_index("fsdp") * piece_len, piece_len, 0)
    emb_piece = lax.all_to_all(emb_grad, "tp", split_axis=0, concat_axis=1, tiled=True).astype(
        jnp.float32
    )
    local_squares = jnp.sum(grad_piece * grad_piece) + jnp.sum(emb_piece * emb_piece)
    gains_local = norm_grad[0, 0]
    gain_sum = lax.psum(gains_local, ("fsdp", "tp"))
    global_squares = lax.psum(local_squares, ("fsdp", "tp"))
    grad_norm = jnp.sqrt(global_squares + jnp.sum(gain_sum * gain_sum))
    clip_factor = jnp.minimum(jnp.float32(1.0), clip_limit / (grad_norm + 1e-06))
    step_value = step_count[0].astype(jnp.float32)
    first_fix = 1.0 - jnp.power(jnp.float32(BETA_ONE), step_value)
    second_fix = 1.0 - jnp.power(jnp.float32(BETA_TWO), step_value)
    flat_new, flat_one, flat_two = adam_update(
        flat_master[0],
        flat_first[0],
        flat_second[0],
        clip_factor * grad_piece,
        first_fix,
        second_fix,
        0.1,
    )
    emb_new, emb_one, emb_two = adam_update(
        emb_master, emb_first, emb_second, clip_factor * emb_piece, first_fix, second_fix, 0.1
    )
    norm_new, norm_one, norm_two = adam_update(
        norm_master, norm_first, norm_second, clip_factor * gain_sum, first_fix, second_fix, 0.0
    )
    gathered = lax.all_gather(flat_new.astype(jnp.bfloat16), "fsdp", axis=0, tiled=True)
    q_weight = gathered[: width * q_columns].reshape(width, q_columns)
    o_weight = gathered[width * q_columns :].reshape(q_columns, width)
    block_rows = width // fsdp_count
    block_start = lax.axis_index("fsdp") * block_rows
    q_block = lax.dynamic_slice_in_dim(q_weight, block_start, block_rows, 0)
    o_block = lax.dynamic_slice_in_dim(o_weight, block_start, block_rows, 1)
    q_average, o_average = (
        lax.all_gather(q_block, "tp", axis=1, tiled=True),
        lax.all_gather(o_block, "tp", axis=0, tiled=True),
    )
    emb_weight = lax.all_to_all(
        emb_new.astype(jnp.bfloat16), "tp", split_axis=1, concat_axis=0, tiled=True
    )
    return (
        flat_new[None, :],
        flat_one[None, :],
        flat_two[None, :],
        emb_new,
        emb_one,
        emb_two,
        norm_new,
        norm_one,
        norm_two,
        q_weight,
        o_weight,
        q_average,
        o_average,
        emb_weight,
    )


def solution(mesh):
    return jax.shard_map(
        body,
        mesh=mesh,
        in_specs=(
            P("fsdp", None, "tp"),
            P("fsdp", "tp", None),
            P("fsdp", "tp", None),
            P("fsdp", "tp"),
            P("tp", "fsdp"),
            P("tp", "fsdp"),
            P("tp", "fsdp"),
            P(("fsdp", "tp"), None),
            P(("fsdp", "tp"), None),
            P(("fsdp", "tp"), None),
            P(),
            P(),
            P(),
            P(),
        ),
        out_specs=(
            P("tp", "fsdp"),
            P("tp", "fsdp"),
            P("tp", "fsdp"),
            P(("fsdp", "tp"), None),
            P(("fsdp", "tp"), None),
            P(("fsdp", "tp"), None),
            P(),
            P(),
            P(),
            P(None, "tp"),
            P("tp", None),
            P("fsdp", None),
            P(None, "fsdp"),
            P("fsdp", "tp"),
        ),
        check_vma=False,
    )
```

profile of v0, /device:TPU:24, one launch (start us, length us, event | category | flops | bytes accessed | tf_op | source)
XLA Modules:
  0.0 419.8 jit_solution(9161934839932907746)
XLA Ops:
  7.2 1.3 copy.56
  8.6 0.8 reshape_squeeze.6
  10.0 1.4 maximum_convert_fusion
  11.4 4.3 %all-to-all-start = ((bf16[4,16,320]{2,1,0:T(8,128)(2,1)}), bf16[4,16,320]{2,1,0:T(8,128)(2,1)S(1)}, u32[]{:S(2)}, u32[]{:S(2)}) async-start(bf16[4,16,320]{2,1,0:T(8,128)(2,1)} %bitcast), calls=%async_computation | async-start | bytes 98304 | tf_op jit(solution)/shard_map/all_to_all | solution.py:51
  16.7 4.6 %all-to-all-done = bf16[4,16,320]{2,1,0:T(8,128)(2,1)S(1)} async-done(((bf16[4,16,320]{2,1,0:T(8,128)(2,1)}), bf16[4,16,320]{2,1,0:T(8,128)(2,1)S(1)}, u32[]{:S(2)}, u32[]{:S(2)}) %all-to-all-start) | async-done | bytes 40992 | tf_op jit(solution)/shard_map/all_to_all | solution.py:51
  21.3 0.6 fusion
  21.9 197.6 %all-reduce.3.cloned.1.call-done = f32[491520]{0:T(1024)} async-done(((f32[491520]{0:T(1024)}), f32[491520]{0:T(1024)}) %all-reduce.3.cloned.1.call-update) | async-done | bytes 1966096 | tf_op jit(solution)/shard_map/psum | solution.py:49
  219.5 1.4 multiply_reduce_fusion
  222.2 95.9 %all-reduce = (f32[]{:T(128)}, f32[1344]{0:T(1024)S(1)}) all-reduce(f32[]{:T(128)S(6)} %add.68, f32[1344]{0:T(1024)S(1)} %reduce.4), channel_id=1, replica_groups=mesh['fsdp'=128,'tp'=4] {'fsdp','tp'}, use_global_device_ids=true, to_apply=%region_3.0 | all-reduce | flops 1345 | bytes 10760 | tf_op jit(solution)/shard_map/psum | solution.py:57
  320.1 0.8 fusion.7
  321.0 51.2 %all-gather = bf16[128,1,3840]{2,1,0:T(2,128)(2,1)S(1)} all-gather(bf16[1,1,3840]{2,1,0:T(2,128)(2,1)S(1)} %reshape.68), channel_id=1, replica_groups=mesh['fsdp'=128,'tp'=4] {'fsdp'}, dimensions={0}, use_global_device_ids=true | all-gather | bytes 990720 | tf_op jit(solution)/shard_map/all_gather | solution.py:78
  372.2 4.3 %slice_reduce_fusion = (bf16[64,3840]{1,0:T(8,128)(2,1)S(1)}, bf16[64,3840]{1,0:T(8,128)(2,1)S(1)}) fusion(bf16[128,1,3840]{2,1,0:T(2,128)(2,1)S(1)} %all-gather), kind=kLoop, calls=%fused_computation | loop fusion | bytes 1966080 | tf_op jit(solution)/shard_map/slice | solution.py:80
  376.5 0.8 slice.27
  377.8 0.7 fusion.5
  378.6 0.6 copy.61
  379.3 3.3 all-to-all-start.1
  382.7 0.6 multiply_subtract_fusion.2
  383.3 1.0 copy.62
  384.3 12.7 %all-gather.1 = bf16[4,192,10]{1,2,0:T(8,128)(2,1)S(1)} all-gather(bf16[1,192,10]{1,2,0:T(8,128)(2,1)S(1)} %dynamic-slice_bitcast_fusion), channel_id=1, replica_groups=mesh['fsdp'=128,'tp'=4] {'tp'}, dimensions={0}, use_global_device_ids=true | all-gather | bytes 19200 | tf_op jit(solution)/shard_map/all_gather | solution.py:86
  397.1 0.7 reshape.71
  397.8 11.9 %all-gather.2 = bf16[4,192,10]{1,2,0:T(8,128)(2,1)S(1)} all-gather(bf16[1,192,10]{1,2,0:T(8,128)(2,1)S(1)} %bitcast.19), channel_id=1, replica_groups=mesh['fsdp'=128,'tp'=4] {'tp'}, dimensions={0}, use_global_device_ids=true | all-gather | bytes 19200 | tf_op jit(solution)/shard_map/all_gather | solution.py:87
  409.8 0.7 reshape.73
  410.5 0.6 broadcast_in_dim.10
  412.3 0.6 copy.66
  (45 shorter events, 3.4 us)
Async XLA Ops:
  7.2 2.2 copy-start.1
  7.2 212.3 %all-reduce.3.cloned.1.call-start = ((), (), s32[]{:S(2)}) async-start(), calls=%async_computation.2 | async-start | bytes 3932160 | tf_op jit(solution)/shard_map/psum | solution.py:49
  9.9 5.8 %copy-start.6 = (f32[1,3840]{1,0:T(1,128)S(1)}, f32[1,3840]{1,0:T(1,128)}, u32[]{:S(2)}) copy-start(f32[1,3840]{1,0:T(1,128)} %param.20) | copy-start | bytes 46084
  9.9 5.8 %copy-start.7 = (f32[1,3840]{1,0:T(1,128)S(1)}, f32[1,3840]{1,0:T(1,128)}, u32[]{:S(2)}) copy-start(f32[1,3840]{1,0:T(1,128)} %param.19) | copy-start | bytes 46084
  10.0 6.6 %copy-start.11 = (f32[1,1,1344]{2,1,0:T(1,128)S(1)}, f32[1,1,1344]{2,1,0:T(1,128)}, u32[]{:S(2)}) copy-start(f32[1,1,1344]{2,1,0:T(1,128)} %param.16) | copy-start | bytes 16132
  10.0 6.6 %copy-start.5 = (f32[1,3840]{1,0:T(1,128)S(1)}, f32[1,3840]{1,0:T(1,128)}, u32[]{:S(2)}) copy-start(f32[1,3840]{1,0:T(1,128)} %param.18) | copy-start | bytes 46084
  11.4 9.8 %all-to-all-start = ((bf16[4,16,320]{2,1,0:T(8,128)(2,1)}), bf16[4,16,320]{2,1,0:T(8,128)(2,1)S(1)}, u32[]{:S(2)}, u32[]{:S(2)}) async-start(bf16[4,16,320]{2,1,0:T(8,128)(2,1)} %bitcast), calls=%async_computation | async-start | bytes 98304 | tf_op jit(solution)/shard_map/all_to_all | solution.py:51
  376.4 1.3 copy-start.2
  376.5 1.3 copy-start.3
  376.5 1.3 copy-start.4
  376.5 6.2 %copy-start.8 = (f32[1344]{0:T(1024)S(1)}, f32[1344]{0:T(1024)}, u32[]{:S(2)}) copy-start(f32[1344]{0:T(1024)} %param.24) | copy-start | bytes 16132
  376.5 6.2 %copy-start.9 = (f32[1344]{0:T(1024)S(1)}, f32[1344]{0:T(1024)}, u32[]{:S(2)}) copy-start(f32[1344]{0:T(1024)} %param.26) | copy-start | bytes 16132
  376.5 6.2 %copy-start.10 = (f32[1344]{0:T(1024)S(1)}, f32[1344]{0:T(1024)}, u32[]{:S(2)}) copy-start(f32[1344]{0:T(1024)} %param.25) | copy-start | bytes 16132
  377.6 35.4 %copy-start = (bf16[192,1280]{1,0:T(8,128)(2,1)}, bf16[192,1280]{1,0:T(8,128)(2,1)S(1)}, u32[]{:S(2)}) copy-start(bf16[192,1280]{1,0:T(8,128)(2,1)S(1)} %slice.29) | copy-start | bytes 1474564
  379.3 33.1 %all-to-all-start.1 = ((bf16[16,4,320]{2,0,1:T(8,128)(2,1)}), bf16[16,4,320]{2,0,1:T(8,128)(2,1)S(1)}, u32[]{:S(2)}, u32[]{:S(2)}) async-start(bf16[16,4,320]{2,0,1:T(8,128)(2,1)} %copy.61), calls=%async_computation.1 | async-start | bytes 98304 | tf_op jit(solution)/shard_map/all_to_all | solution.py:89
Sparse Core Ops, SparseCore 0:
  11.5 207.9 all-reduce.2
where the time goes:
time: 420 us
  waiting for transfers between devices  202 us (48%)
  blocking collectives  172 us (41%)
  between operations  17.7 us (4%)
  local copies, waits for them, and re-layouts  14 us (3%)
  starting transfers between devices  7.62 us (2%)
  other arithmetic  6.4 us (2%)
    psum x1, waiting for transfers between devices, body(): summed = lax.psum(local_flat.astype(jnp.float32), 'fsdp')  198 us
    psum x1, blocking collectives, body(): global_squares = lax.psum(local_squares, ('fsdp', 'tp'))  95.9 us
    all_gather x1, blocking collectives, body(): lax.all_gather(flat_new.astype(jnp.bfloat16), 'fsdp', axis=0, tiled=True)  51.2 us
    all_gather x1, blocking collectives, body(): lax.all_gather(q_block, 'tp', axis=1, tiled=True)  12.7 us
    all_gather x1, blocking collectives, body(): lax.all_gather(o_block, 'tp', axis=0, tiled=True)  11.9 us
  transfers between devices with their start and end apart: 3, of which 2 were waited for; matrix products, arithmetic and copies ran while one was open for 1% of the time, Pallas kernels for 0%

commit v1 on v0

--- a/solution.py
+++ b/solution.py
@@ -84,7 +84,9 @@
     o_block = lax.dynamic_slice_in_dim(o_weight, block_start, block_rows, 1)
     q_average, o_average = (
         lax.all_gather(q_block, "tp", axis=1, tiled=True),
-        lax.all_gather(o_block, "tp", axis=0, tiled=True),
+        jnp.concatenate(
+            lax.all_to_all(jnp.stack([o_block] * lax.axis_size("tp")), "tp", 0, 0), axis=0
+        ),
     )
     emb_weight = lax.all_to_all(
         emb_new.astype(jnp.bfloat16), "tp", split_axis=1, concat_axis=0, tiled=True

time: 420 us -> 415 us (0.988)
  blocking collectives: 172 us -> 160 us
    all_gather x1 -> x0, blocking collectives: 11.9 us -> none  [body(): lax.all_gather(o_block, 'tp', axis=0, tiled=True)]
  transfers between devices with their start and end apart: 3 -> 4, of which waited for: 2 -> 3; matrix products, arithmetic and copies ran while one was open for 1% -> 2% of each run, Pallas kernels for 0% -> 0%
where the time goes in v1:
time: 415 us; the launch traced here: 414 us
  waiting for transfers between devices  204 us (49%)
  blocking collectives  160 us (39%)
  between operations  17.7 us (4%)
  local copies, waits for them, and re-layouts  14.8 us (4%)
  starting transfers between devices  10.9 us (3%)
  other arithmetic  6.39 us (2%)
    psum x1, waiting for transfers between devices, body(): summed = lax.psum(local_flat.astype(jnp.float32), 'fsdp')  198 us
    psum x1, blocking collectives, body(): global_squares = lax.psum(local_squares, ('fsdp', 'tp'))  95.9 us
    all_gather x1, blocking collectives, body(): lax.all_gather(flat_new.astype(jnp.bfloat16), 'fsdp', axis=0, tiled=True)  51.2 us
    all_gather x1, blocking collectives, body(): lax.all_gather(q_block, 'tp', axis=1, tiled=True)  12.7 us
  transfers between devices with their start and end apart: 4, of which 3 were waited for; matrix products, arithmetic and copies ran while one was open for 2% of the time, Pallas kernels for 0%

profile of v1, /device:TPU:24, one launch (start us, length us, event | category | flops | bytes accessed | tf_op | source)
XLA Modules:
  0.0 414.1 jit_solution(1278587095123389375)
XLA Ops:
  7.2 1.3 copy.55
  8.6 0.8 reshape_squeeze.6
  10.0 1.4 maximum_convert_fusion
  11.4 4.3 %all-to-all-start = ((bf16[4,16,320]{2,1,0:T(8,128)(2,1)}), bf16[4,16,320]{2,1,0:T(8,128)(2,1)S(1)}, u32[]{:S(2)}, u32[]{:S(2)}) async-start(bf16[4,16,320]{2,1,0:T(8,128)(2,1)} %bitcast), calls=%async_computation | async-start | bytes 98304 | tf_op jit(solution)/shard_map/all_to_all | solution.py:51
  16.7 4.6 %all-to-all-done = bf16[4,16,320]{2,1,0:T(8,128)(2,1)S(1)} async-done(((bf16[4,16,320]{2,1,0:T(8,128)(2,1)}), bf16[4,16,320]{2,1,0:T(8,128)(2,1)S(1)}, u32[]{:S(2)}, u32[]{:S(2)}) %all-to-all-start) | async-done | bytes 40992 | tf_op jit(solution)/shard_map/all_to_all | solution.py:51
  21.3 0.6 fusion
  21.9 197.6 %all-reduce.3.cloned.1.call-done = f32[491520]{0:T(1024)} async-done(((f32[491520]{0:T(1024)}), f32[491520]{0:T(1024)}) %all-reduce.3.cloned.1.call-update) | async-done | bytes 1966096 | tf_op jit(solution)/shard_map/psum | solution.py:49
  219.5 1.4 multiply_reduce_fusion
  222.2 95.9 %all-reduce = (f32[]{:T(128)}, f32[1344]{0:T(1024)S(1)}) all-reduce(f32[]{:T(128)S(6)} %add.68, f32[1344]{0:T(1024)S(1)} %reduce.4), channel_id=1, replica_groups=mesh['fsdp'=128,'tp'=4] {'fsdp','tp'}, use_global_device_ids=true, to_apply=%region_3.0 | all-reduce | flops 1345 | bytes 10760 | tf_op jit(solution)/shard_map/psum | solution.py:57
  320.1 0.8 fusion.7
  321.0 51.2 %all-gather = bf16[128,1,3840]{2,1,0:T(2,128)(2,1)S(1)} all-gather(bf16[1,1,3840]{2,1,0:T(2,128)(2,1)S(1)} %reshape.74), channel_id=1, replica_groups=mesh['fsdp'=128,'tp'=4] {'fsdp'}, dimensions={0}, use_global_device_ids=true | all-gather | bytes 990720 | tf_op jit(solution)/shard_map/all_gather | solution.py:78
  372.2 4.3 %slice_reduce_fusion = (bf16[64,3840]{1,0:T(8,128)(2,1)S(1)}, bf16[64,3840]{1,0:T(8,128)(2,1)S(1)}) fusion(bf16[128,1,3840]{2,1,0:T(2,128)(2,1)S(1)} %all-gather), kind=kLoop, calls=%fused_computation | loop fusion | bytes 1966080 | tf_op jit(solution)/shard_map/slice | solution.py:80
  376.9 0.7 reshape.88
  377.7 3.3 all-to-all-start.1
  381.1 0.7 fusion.5
  381.9 0.6 multiply_subtract_fusion.2
  382.5 0.8 slice.27
  383.4 0.6 copy.60
  384.0 2.2 all-to-all-done.1
  386.2 3.3 all-to-all-start.2
  389.6 1.0 copy.61
  390.6 12.7 %all-gather.1 = bf16[4,192,10]{1,2,0:T(8,128)(2,1)S(1)} all-gather(bf16[1,192,10]{1,2,0:T(8,128)(2,1)S(1)} %dynamic-slice_bitcast_fusion), channel_id=1, replica_groups=mesh['fsdp'=128,'tp'=4] {'tp'}, dimensions={0}, use_global_device_ids=true | all-gather | bytes 19200 | tf_op jit(solution)/shard_map/all_gather | solution.py:86
  403.3 0.7 reshape.77
  405.9 0.7 reshape.73
  (49 shorter events, 4.8 us)
Async XLA Ops:
  7.2 2.2 copy-start.1
  7.2 212.3 %all-reduce.3.cloned.1.call-start = ((), (), s32[]{:S(2)}) async-start(), calls=%async_computation.3 | async-start | bytes 3932160 | tf_op jit(solution)/shard_map/psum | solution.py:49
  9.9 5.8 %copy-start.6 = (f32[1,3840]{1,0:T(1,128)S(1)}, f32[1,3840]{1,0:T(1,128)}, u32[]{:S(2)}) copy-start(f32[1,3840]{1,0:T(1,128)} %param.20) | copy-start | bytes 46084
  9.9 5.8 %copy-start.7 = (f32[1,3840]{1,0:T(1,128)S(1)}, f32[1,3840]{1,0:T(1,128)}, u32[]{:S(2)}) copy-start(f32[1,3840]{1,0:T(1,128)} %param.19) | copy-start | bytes 46084
  10.0 6.6 %copy-start.11 = (f32[1,1,1344]{2,1,0:T(1,128)S(1)}, f32[1,1,1344]{2,1,0:T(1,128)}, u32[]{:S(2)}) copy-start(f32[1,1,1344]{2,1,0:T(1,128)} %param.16) | copy-start | bytes 16132
  10.0 6.6 %copy-start.5 = (f32[1,3840]{1,0:T(1,128)S(1)}, f32[1,3840]{1,0:T(1,128)}, u32[]{:S(2)}) copy-start(f32[1,3840]{1,0:T(1,128)} %param.18) | copy-start | bytes 46084
  11.4 9.8 %all-to-all-start = ((bf16[4,16,320]{2,1,0:T(8,128)(2,1)}), bf16[4,16,320]{2,1,0:T(8,128)(2,1)S(1)}, u32[]{:S(2)}, u32[]{:S(2)}) async-start(bf16[4,16,320]{2,1,0:T(8,128)(2,1)} %bitcast), calls=%async_computation | async-start | bytes 98304 | tf_op jit(solution)/shard_map/all_to_all | solution.py:51
  372.2 8.9 %copy-start.2 = (f32[16,1280]{1,0:T(8,128)S(1)}, f32[16,1280]{1,0:T(8,128)}, u32[]{:S(2)}) copy-start(f32[16,1280]{1,0:T(8,128)} %param.21) | copy-start | bytes 245764
  372.2 8.9 %copy-start.3 = (f32[16,1280]{1,0:T(8,128)S(1)}, f32[16,1280]{1,0:T(8,128)}, u32[]{:S(2)}) copy-start(f32[16,1280]{1,0:T(8,128)} %param.23) | copy-start | bytes 245764
  372.2 8.9 %copy-start.4 = (f32[16,1280]{1,0:T(8,128)S(1)}, f32[16,1280]{1,0:T(8,128)}, u32[]{:S(2)}) copy-start(f32[16,1280]{1,0:T(8,128)} %param.22) | copy-start | bytes 245764
  372.2 9.7 %copy-start.8 = (f32[1344]{0:T(1024)S(1)}, f32[1344]{0:T(1024)}, u32[]{:S(2)}) copy-start(f32[1344]{0:T(1024)} %param.24) | copy-start | bytes 16132
  372.2 9.7 %copy-start.9 = (f32[1344]{0:T(1024)S(1)}, f32[1344]{0:T(1024)}, u32[]{:S(2)}) copy-start(f32[1344]{0:T(1024)} %param.26) | copy-start | bytes 16132
  372.2 9.7 %copy-start.10 = (f32[1344]{0:T(1024)S(1)}, f32[1344]{0:T(1024)}, u32[]{:S(2)}) copy-start(f32[1344]{0:T(1024)} %param.25) | copy-start | bytes 16132
  376.7 13.8 %copy-start = (bf16[192,1280]{1,0:T(8,128)(2,1)}, bf16[192,1280]{1,0:T(8,128)(2,1)S(1)}, u32[]{:S(2)}) copy-start(bf16[192,1280]{1,0:T(8,128)(2,1)S(1)} %slice.29) | copy-start | bytes 1474564
  377.7 8.6 %all-to-all-start.1 = ((bf16[4,2,960]{2,1,0:T(2,128)(2,1)}), bf16[4,2,960]{2,1,0:T(2,128)(2,1)S(1)}, u32[]{:S(2)}, u32[]{:S(2)}) async-start(bf16[4,2,960]{2,1,0:T(2,128)(2,1)} %reshape.88), calls=%async_computation.1 | async-start | bytes 32768 | tf_op jit(solution)/shard_map/all_to_all | solution.py:88
  386.2 20.4 %all-to-all-start.2 = ((bf16[16,4,320]{2,0,1:T(8,128)(2,1)}), bf16[16,4,320]{2,0,1:T(8,128)(2,1)S(1)}, u32[]{:S(2)}, u32[]{:S(2)}) async-start(bf16[16,4,320]{2,0,1:T(8,128)(2,1)} %copy.60), calls=%async_computation.2 | async-start | bytes 98304 | tf_op jit(solution)/shard_map/all_to_all | solution.py:91
Sparse Core Ops, SparseCore 0:
  11.5 207.9 all-reduce.2
